TPU v7x, 32 devices: a whole 2x2x4 slice. The times are simulated.
32 devices in a mesh: mem: 4 (over y, core), row: 8 (over z, x).
Axes of the slice: x: 2, y: 2, z: 4, core: 2. Of those that a mesh axis runs over, the one named last changes fastest.
Arguments:
- starting_states: float32 [8, 8, 64, 512], P('mem', None, 'row'), may hold values from -6 to 6
- wind_east: float32 [8, 64, 512], P(None, 'row'), may hold values from -0.25 to 0.25
- wind_north: float32 [8, 64, 512], P(None, 'row'), may hold values from -0.25 to 0.25
- diffusivity: float32 [8, 64, 512], P(None, 'row'), may hold values from 0.05 to 0.22
- embed_weight: bfloat16 [8, 64], replicated, may hold values from -2 to 2
- norm_gain: float32 [64], replicated, may hold values from 0.1 to 1.9
- project_weight: bfloat16 [64, 192], replicated, may hold values from -0.75 to 0.75
- head_scale: float32 [4], replicated, may hold values from 1 to 10
- output_weight: bfloat16 [64, 64], replicated, may hold values from -0.75 to 0.75
- readout_weight: bfloat16 [64, 8], replicated, may hold values from -0.75 to 0.75
- first_kernel: bfloat16 [9, 8, 8], replicated, may hold values from -0.75 to 0.75
- second_kernel: bfloat16 [9, 8, 8], replicated, may hold values from -0.75 to 0.75
Outputs:
- postprocessed: bfloat16 [8, 8, 64, 512], P(None, None, 'row', 'mem')
All inputs are finite; a program needn't handle non-finite values.
Results may differ from a plain program's by a relative error of at most 0.0096.
Values may be sent and summed in bfloat16 or wider, within the bound.
No kernel may reach another device: no remote copies, remote signals or barrier semaphores. Data moves between devices by JAX's collectives and lax.ppermute only.
A program may use at most 64 MiB of HBM per device.

v0:
```python
import jax
import jax.numpy as jnp
from jax import lax
from jax.sharding import PartitionSpec as P

STEPS = 4
DILATION_SPAN = 4


def padded(block, sides, width):
    for axis, dim in sides:
        count = lax.axis_size(axis)
        forward = [(i, i + 1) for i in range(count - 1)]
        backward = [(target, source) for source, target in forward]
        low = lax.ppermute(
            lax.slice_in_dim(block, block.shape[dim] - width, None, axis=dim), axis, forward
        )
        high = lax.ppermute(lax.slice_in_dim(block, 0, width, axis=dim), axis, backward)
        block = jnp.concatenate([low, block, high], axis=dim)
    return block


def advance(padded_field, wind_east, wind_north, diffusivity):
    middle = padded_field[..., 1:-1, :]
    northern = padded_field[..., 2:, :]
    southern = padded_field[..., :-2, :]
    widths = [(0, 0)] * (middle.ndim - 1) + [(1, 1)]
    widened = jnp.pad(middle, widths)
    eastern = widened[..., 2:]
    western = widened[..., :-2]
    drifting = 0.2 * jnp.tanh(middle)
    laplace = northern + southern + eastern + western - 4.0 * middle
    return (
        middle
        - (wind_east + drifting) * (eastern - western) * 0.5
        - (wind_north + drifting) * (northern - southern) * 0.5
        + diffusivity * laplace
    )


def post_block(
    vertical_layers,
    embed_weight,
    norm_gain,
    project_weight,
    head_scale,
    output_weight,
    readout_weight,
):
    members, _, points = vertical_layers.shape
    width = embed_weight.shape[1]
    heads = head_scale.shape[0]
    head_size = width // heads
    embedded = jnp.einsum(
        "mlp,le->pme", vertical_layers, embed_weight, preferred_element_type=jnp.float32
    )
    meansq = jnp.mean(embedded * embedded, axis=-1, keepdims=True)
    normed = (embedded * lax.rsqrt(meansq + 1e-05) * norm_gain).astype(jnp.bfloat16)
    projected = jnp.einsum(
        "pme,ef->pmf", normed, project_weight, preferred_element_type=jnp.float32
    )
    queries = projected[..., :width].reshape(points, members, heads, head_size)
    keys_all = projected[..., width : 2 * width].reshape(points, members, heads, head_size)
    values = (
        projected[..., 2 * width :].astype(jnp.bfloat16).reshape(points, members, heads, head_size)
    )
    queries = (queries * lax.rsqrt(jnp.sum(queries * queries, -1, keepdims=True) + 1.0)).astype(
        jnp.bfloat16
    )
    keys_all = (keys_all * lax.rsqrt(jnp.sum(keys_all * keys_all, -1, keepdims=True) + 1.0)).astype(
        jnp.bfloat16
    )
    scores = jnp.einsum("pmhd,pnhd->phmn", queries, keys_all, preferred_element_type=jnp.float32)
    scores = scores * head_scale[:, None, None]
    weights = jnp.exp(scores)
    probs = (weights / jnp.sum(weights, -1, keepdims=True)).astype(jnp.bfloat16)
    mixed = jnp.einsum("phmn,pnhd->pmhd", probs, values, preferred_element_type=jnp.float32)
    mixed = mixed.astype(jnp.bfloat16).reshape(points, members, width)
    attended = jnp.einsum("pme,ef->pmf", mixed, output_weight, preferred_element_type=jnp.float32)
    residual = (embedded + attended).astype(jnp.bfloat16)
    step_result = jnp.einsum(
        "pme,ef->mfp", residual, readout_weight, preferred_element_type=jnp.float32
    )
    return step_result.astype(jnp.bfloat16)


def convolve(padded_field, kernel):
    row_total = padded_field.shape[2] - 2 * DILATION_SPAN
    column_total = padded_field.shape[3] - 2 * DILATION_SPAN
    summed = jnp.zeros(
        (padded_field.shape[0], kernel.shape[1], row_total, column_total), jnp.float32
    )
    for row_stencil in range(3):
        for column_stencil in range(3):
            shifted_field = padded_field[
                :,
                :,
                row_stencil * DILATION_SPAN : row_stencil * DILATION_SPAN + row_total,
                column_stencil * DILATION_SPAN : column_stencil * DILATION_SPAN + column_total,
            ]
            summed = summed + jnp.einsum(
                "oc,mcij->moij",
                kernel[row_stencil * 3 + column_stencil],
                shifted_field,
                preferred_element_type=jnp.float32,
            )
    return summed


def on_device(
    starting_states,
    wind_east,
    wind_north,
    diffusivity,
    embed_weight,
    norm_gain,
    project_weight,
    head_scale,
    output_weight,
    readout_weight,
    first_kernel,
    second_kernel,
):
    members_here = starting_states.shape[0]
    row_total = starting_states.shape[2]
    coefficients = jnp.stack([wind_east, wind_north, diffusivity])
    joined = jnp.concatenate([starting_states, coefficients], 0)
    widened = padded(joined, (("row", 2),), STEPS)
    gridded_quantity_list = widened[:members_here]
    coef_rows = widened[members_here:]
    first_row = lax.axis_index("row") * row_total - STEPS
    all_rows = lax.axis_size("row") * row_total
    for section in range(STEPS):
        out_rows = row_total + 2 * (STEPS - section - 1)
        offset = section + 1
        window = coef_rows[:, :, offset : offset + out_rows]
        gridded_quantity_list = advance(gridded_quantity_list, window[0], window[1], window[2])
        row_ids = first_row + offset + jnp.arange(out_rows)
        inside = (row_ids >= 0) & (row_ids < all_rows)
        gridded_quantity_list = jnp.where(inside[None, None, :, None], gridded_quantity_list, 0.0)
    predicted_states = gridded_quantity_list.astype(jnp.bfloat16)
    blockwise_quantity = lax.all_to_all(
        predicted_states, "mem", split_axis=3, concat_axis=0, tiled=True
    )
    members, levels_count, tile_rows, tile_cols = blockwise_quantity.shape
    count = tile_rows * tile_cols
    flattened = blockwise_quantity.reshape(members, levels_count, count)
    block = 256

    def one_block(block_index):
        vertical_layers = lax.dynamic_slice_in_dim(flattened, block_index * block, block, 2)
        return post_block(
            vertical_layers,
            embed_weight,
            norm_gain,
            project_weight,
            head_scale,
            output_weight,
            readout_weight,
        )

    blocks = lax.map(one_block, jnp.arange(count // block))
    step_result = jnp.moveaxis(blocks, 0, 2)
    features = step_result.reshape(members, readout_weight.shape[1], tile_rows, tile_cols)
    tile_cols = features.shape[3]
    padded_feature = padded(features, (("mem", 3), ("row", 2)), DILATION_SPAN)
    interior_cells = jax.nn.silu(convolve(padded_feature, first_kernel)).astype(jnp.bfloat16)
    activated_output = padded(interior_cells, (("mem", 3), ("row", 2)), DILATION_SPAN)
    return (features.astype(jnp.float32) + convolve(activated_output, second_kernel)).astype(
        jnp.bfloat16
    )


def solution(mesh):
    return jax.shard_map(
        on_device,
        mesh=mesh,
        in_specs=(
            P("mem", None, "row", None),
            P(None, "row", None),
            P(None, "row", None),
            P(None, "row", None),
            P(),
            P(),
            P(),
            P(),
            P(),
            P(),
            P(),
            P(),
        ),
        out_specs=P(None, None, "row", "mem"),
        check_vma=False,
    )
```

profile of v0, /device:TPU:1, one launch (start us, length us, event | category | flops | bytes accessed | tf_op | source)
XLA Modules:
  0.0 220.1 jit_solution(953675717168693512)
XLA Ops:
  0.0 1.0 copy.200
  1.0 1.1 copy.121
  2.1 1.1 fusion.90
  3.4 4.0 %collective-permute-start = (f32[5,8,4,512]{3,1,2,0:T(8,128)S(1)}, f32[5,8,4,512]{3,1,2,0:T(8,128)S(1)}, u32[]{:S(2)}, u32[]{:S(2)}) collective-permute-start(f32[5,8,4,512]{3,1,2,0:T(8,128)S(1)} %get-tuple-element.115), channel_id=1, source_target_pairs={{0,1},{1,2},{2,3},{3,4},{4,5},{5,6},{6,7},{8,9},{9,10},{10,11},{11... | collective-permute-start | bytes 983048 | tf_op jit(solution)/shard_map/ppermute | solution.py:15
  7.3 1.3 collective-permute-start.1
  8.8 11.9 %collective-permute-done = f32[5,8,4,512]{3,1,2,0:T(8,128)S(1)} collective-permute-done((f32[5,8,4,512]{3,1,2,0:T(8,128)S(1)}, f32[5,8,4,512]{3,1,2,0:T(8,128)S(1)}, u32[]{:S(2)}, u32[]{:S(2)}) %collective-permute-start) | collective-permute-done | bytes 327712 | tf_op jit(solution)/shard_map/ppermute | solution.py:15
  21.0 0.5 add_select_fusion
  22.7 2.0 copy.125
  24.7 2.8 %reshape.99 = bf16[4,2,8192]{2,1,0:T(2,128)(2,1)} reshape(bf16[512,2,8,8]{3,2,1,0:T(8,128)(2,1)S(1)} %bitcast.241) | data formatting | bytes 262144
  27.6 4.8 %all-to-all-start = ((bf16[4,2,8192]{2,1,0:T(2,128)(2,1)}), bf16[4,2,8192]{2,1,0:T(2,128)(2,1)S(1)}, u32[]{:S(2)}, u32[]{:S(2)}) async-start(bf16[4,2,8192]{2,1,0:T(2,128)(2,1)} %reshape.99), calls=%async_computation | async-start | bytes 262144 | tf_op jit(solution)/shard_map/all_to_all | solution.py:142
  35.1 0.9 all-to-all-done
  36.0 2.4 %reshape.100 = bf16[512,2,8,8]{3,2,1,0:T(8,128)(2,1)S(1)} reshape(bf16[4,2,8192]{2,1,0:T(2,128)(2,1)S(1)} %all-to-all-done) | data formatting | bytes 262144
  38.4 1.7 copy.126
  40.2 135.4 %while.10 = (s32[]{:T(128)}, bf16[4,8,8,256]{3,2,1,0:T(8,128)(2,1)S(1)}, s32[4]{0:T(128)S(1)}, bf16[8,8,1024]{2,1,0:T(8,128)(2,1)S(1)}, bf16[8,64]{1,0:T(8,128)(...) while((s32[]{:T(128)}, ...), condition=%wide.region_5.6_spmd, body=%wide.region_0.5_spmd.sunk | while | flops 77932544 | bytes 12530179 | solution.py:162
  40.4 0.6 dynamic_slice.14
  42.8 3.7 %copy.208 = bf16[256,8,4,16]{3,1,2,0:T(8,128)(2,1)} copy(bf16[256,8,4,16]{0,3,2,1:T(8,128)(2,1)S(1)} %get-tuple-element.230) | data formatting | bytes 524288 | tf_op jit(solution)/shard_map/while/body/eval_jaxpr/convert_element_type | solution.py:67
  46.5 3.8 %copy.209 = bf16[256,8,4,16]{3,1,2,0:T(8,128)(2,1)} copy(bf16[256,8,4,16]{0,3,2,1:T(8,128)(2,1)S(1)} %get-tuple-element.231) | data formatting | bytes 524288 | tf_op jit(solution)/shard_map/while/body/eval_jaxpr/convert_element_type | solution.py:70
  50.3 5.4 %fusion.123 = f32[256,4,8,8]{2,3,1,0:T(8,128)} fusion(bf16[256,8,4,16]{3,1,2,0:T(8,128)(2,1)} %copy.208, bf16[256,8,4,16]{3,1,2,0:T(8,128)(2,1)} %copy.209), kind=kOutput, calls=%fused_computation.154.clone.1 | convolution fusion | flops 2097152 | bytes 786432 | tf_op jit(solution)/shard_map/while/body/eval_jaxpr/pmhd,pnhd->phmn/dot_general | solution.py:73
  55.7 3.6 %copy.210 = f32[256,4,8,8]{0,3,2,1:T(8,128)S(1)} copy(f32[256,4,8,8]{2,3,1,0:T(8,128)} %fusion.123) | data formatting | bytes 524288 | tf_op jit(solution)/shard_map/while/body/eval_jaxpr/pmhd,pnhd->phmn/dot_general | solution.py:73
  59.6 3.7 %copy.211 = bf16[256,4,8,8]{3,2,1,0:T(8,128)(2,1)} copy(bf16[256,4,8,8]{0,3,2,1:T(8,128)(2,1)S(1)} %divide_convert_fusion.2) | data formatting | bytes 262144 | tf_op jit(solution)/shard_map/while/body/eval_jaxpr/convert_element_type | solution.py:76
  63.2 3.7 %copy.207 = bf16[256,8,4,16]{3,1,2,0:T(8,128)(2,1)} copy(bf16[256,8,4,16]{0,3,2,1:T(8,128)(2,1)S(1)} %bitcast.240) | data formatting | bytes 524288 | tf_op jit(solution)/shard_map/while/body/eval_jaxpr/reshape | solution.py:65
  66.9 4.1 %convert_bitcast_fusion.2 = bf16[256,8,4,16]{3,1,2,0:T(8,128)(2,1)} fusion(bf16[256,8,4,16]{3,1,2,0:T(8,128)(2,1)} %copy.207, bf16[256,4,8,8]{3,2,1,0:T(8,128)(2,1)S(1)} %copy-done), kind=kOutput, calls=%fused_computation.clone.1 | convolution fusion | flops 2228224 | bytes 655360 | tf_op jit(solution)/shard_map/while/body/eval_jaxpr/phmn,pnhd->pmhd/dot_general | solution.py:77
  71.1 2.7 %copy.212 = bf16[256,8,4,16]{0,3,2,1:T(8,128)(2,1)S(1)} copy(bf16[256,8,4,16]{3,1,2,0:T(8,128)(2,1)} %convert_bitcast_fusion.2) | data formatting | bytes 524288 | tf_op jit(solution)/shard_map/while/body/eval_jaxpr/convert_element_type | solution.py:78
  74.1 0.6 dynamic_slice.14
  76.6 3.7 %copy.208 = bf16[256,8,4,16]{3,1,2,0:T(8,128)(2,1)} copy(bf16[256,8,4,16]{0,3,2,1:T(8,128)(2,1)S(1)} %get-tuple-element.230) | data formatting | bytes 524288 | tf_op jit(solution)/shard_map/while/body/eval_jaxpr/convert_element_type | solution.py:67
  80.3 3.8 %copy.209 = bf16[256,8,4,16]{3,1,2,0:T(8,128)(2,1)} copy(bf16[256,8,4,16]{0,3,2,1:T(8,128)(2,1)S(1)} %get-tuple-element.231) | data formatting | bytes 524288 | tf_op jit(solution)/shard_map/while/body/eval_jaxpr/convert_element_type | solution.py:70
  84.1 5.4 %fusion.123 = f32[256,4,8,8]{2,3,1,0:T(8,128)} fusion(bf16[256,8,4,16]{3,1,2,0:T(8,128)(2,1)} %copy.208, bf16[256,8,4,16]{3,1,2,0:T(8,128)(2,1)} %copy.209), kind=kOutput, calls=%fused_computation.154.clone.1 | convolution fusion | flops 2097152 | bytes 786432 | tf_op jit(solution)/shard_map/while/body/eval_jaxpr/pmhd,pnhd->phmn/dot_general | solution.py:73
  89.5 3.6 %copy.210 = f32[256,4,8,8]{0,3,2,1:T(8,128)S(1)} copy(f32[256,4,8,8]{2,3,1,0:T(8,128)} %fusion.123) | data formatting | bytes 524288 | tf_op jit(solution)/shard_map/while/body/eval_jaxpr/pmhd,pnhd->phmn/dot_general | solution.py:73
  93.3 3.7 %copy.211 = bf16[256,4,8,8]{3,2,1,0:T(8,128)(2,1)} copy(bf16[256,4,8,8]{0,3,2,1:T(8,128)(2,1)S(1)} %divide_convert_fusion.2) | data formatting | bytes 262144 | tf_op jit(solution)/shard_map/while/body/eval_jaxpr/convert_element_type | solution.py:76
  97.0 3.7 %copy.207 = bf16[256,8,4,16]{3,1,2,0:T(8,128)(2,1)} copy(bf16[256,8,4,16]{0,3,2,1:T(8,128)(2,1)S(1)} %bitcast.240) | data formatting | bytes 524288 | tf_op jit(solution)/shard_map/while/body/eval_jaxpr/reshape | solution.py:65
  100.7 4.1 %convert_bitcast_fusion.2 = bf16[256,8,4,16]{3,1,2,0:T(8,128)(2,1)} fusion(bf16[256,8,4,16]{3,1,2,0:T(8,128)(2,1)} %copy.207, bf16[256,4,8,8]{3,2,1,0:T(8,128)(2,1)S(1)} %copy-done), kind=kOutput, calls=%fused_computation.clone.1 | convolution fusion | flops 2228224 | bytes 655360 | tf_op jit(solution)/shard_map/while/body/eval_jaxpr/phmn,pnhd->pmhd/dot_general | solution.py:77
  104.9 2.7 %copy.212 = bf16[256,8,4,16]{0,3,2,1:T(8,128)(2,1)S(1)} copy(bf16[256,8,4,16]{3,1,2,0:T(8,128)(2,1)} %convert_bitcast_fusion.2) | data formatting | bytes 524288 | tf_op jit(solution)/shard_map/while/body/eval_jaxpr/convert_element_type | solution.py:78
  107.9 0.6 dynamic_slice.14
  110.4 3.7 %copy.208 = bf16[256,8,4,16]{3,1,2,0:T(8,128)(2,1)} copy(bf16[256,8,4,16]{0,3,2,1:T(8,128)(2,1)S(1)} %get-tuple-element.230) | data formatting | bytes 524288 | tf_op jit(solution)/shard_map/while/body/eval_jaxpr/convert_element_type | solution.py:67
  114.1 3.8 %copy.209 = bf16[256,8,4,16]{3,1,2,0:T(8,128)(2,1)} copy(bf16[256,8,4,16]{0,3,2,1:T(8,128)(2,1)S(1)} %get-tuple-element.231) | data formatting | bytes 524288 | tf_op jit(solution)/shard_map/while/body/eval_jaxpr/convert_element_type | solution.py:70
  117.9 5.4 %fusion.123 = f32[256,4,8,8]{2,3,1,0:T(8,128)} fusion(bf16[256,8,4,16]{3,1,2,0:T(8,128)(2,1)} %copy.208, bf16[256,8,4,16]{3,1,2,0:T(8,128)(2,1)} %copy.209), kind=kOutput, calls=%fused_computation.154.clone.1 | convolution fusion | flops 2097152 | bytes 786432 | tf_op jit(solution)/shard_map/while/body/eval_jaxpr/pmhd,pnhd->phmn/dot_general | solution.py:73
  123.3 3.6 %copy.210 = f32[256,4,8,8]{0,3,2,1:T(8,128)S(1)} copy(f32[256,4,8,8]{2,3,1,0:T(8,128)} %fusion.123) | data formatting | bytes 524288 | tf_op jit(solution)/shard_map/while/body/eval_jaxpr/pmhd,pnhd->phmn/dot_general | solution.py:73
  127.1 3.7 %copy.211 = bf16[256,4,8,8]{3,2,1,0:T(8,128)(2,1)} copy(bf16[256,4,8,8]{0,3,2,1:T(8,128)(2,1)S(1)} %divide_convert_fusion.2) | data formatting | bytes 262144 | tf_op jit(solution)/shard_map/while/body/eval_jaxpr/convert_element_type | solution.py:76
  130.8 3.7 %copy.207 = bf16[256,8,4,16]{3,1,2,0:T(8,128)(2,1)} copy(bf16[256,8,4,16]{0,3,2,1:T(8,128)(2,1)S(1)} %bitcast.240) | data formatting | bytes 524288 | tf_op jit(solution)/shard_map/while/body/eval_jaxpr/reshape | solution.py:65
  134.5 4.1 %convert_bitcast_fusion.2 = bf16[256,8,4,16]{3,1,2,0:T(8,128)(2,1)} fusion(bf16[256,8,4,16]{3,1,2,0:T(8,128)(2,1)} %copy.207, bf16[256,4,8,8]{3,2,1,0:T(8,128)(2,1)S(1)} %copy-done), kind=kOutput, calls=%fused_computation.clone.1 | convolution fusion | flops 2228224 | bytes 655360 | tf_op jit(solution)/shard_map/while/body/eval_jaxpr/phmn,pnhd->pmhd/dot_general | solution.py:77
  138.6 2.7 %copy.212 = bf16[256,8,4,16]{0,3,2,1:T(8,128)(2,1)S(1)} copy(bf16[256,8,4,16]{3,1,2,0:T(8,128)(2,1)} %convert_bitcast_fusion.2) | data formatting | bytes 524288 | tf_op jit(solution)/shard_map/while/body/eval_jaxpr/convert_element_type | solution.py:78
  141.7 0.6 dynamic_slice.14
  144.1 3.7 %copy.208 = bf16[256,8,4,16]{3,1,2,0:T(8,128)(2,1)} copy(bf16[256,8,4,16]{0,3,2,1:T(8,128)(2,1)S(1)} %get-tuple-element.230) | data formatting | bytes 524288 | tf_op jit(solution)/shard_map/while/body/eval_jaxpr/convert_element_type | solution.py:67
  147.9 3.8 %copy.209 = bf16[256,8,4,16]{3,1,2,0:T(8,128)(2,1)} copy(bf16[256,8,4,16]{0,3,2,1:T(8,128)(2,1)S(1)} %get-tuple-element.231) | data formatting | bytes 524288 | tf_op jit(solution)/shard_map/while/body/eval_jaxpr/convert_element_type | solution.py:70
  151.7 5.4 %fusion.123 = f32[256,4,8,8]{2,3,1,0:T(8,128)} fusion(bf16[256,8,4,16]{3,1,2,0:T(8,128)(2,1)} %copy.208, bf16[256,8,4,16]{3,1,2,0:T(8,128)(2,1)} %copy.209), kind=kOutput, calls=%fused_computation.154.clone.1 | convolution fusion | flops 2097152 | bytes 786432 | tf_op jit(solution)/shard_map/while/body/eval_jaxpr/pmhd,pnhd->phmn/dot_general | solution.py:73
  157.1 3.6 %copy.210 = f32[256,4,8,8]{0,3,2,1:T(8,128)S(1)} copy(f32[256,4,8,8]{2,3,1,0:T(8,128)} %fusion.123) | data formatting | bytes 524288 | tf_op jit(solution)/shard_map/while/body/eval_jaxpr/pmhd,pnhd->phmn/dot_general | solution.py:73
  160.9 3.7 %copy.211 = bf16[256,4,8,8]{3,2,1,0:T(8,128)(2,1)} copy(bf16[256,4,8,8]{0,3,2,1:T(8,128)(2,1)S(1)} %divide_convert_fusion.2) | data formatting | bytes 262144 | tf_op jit(solution)/shard_map/while/body/eval_jaxpr/convert_element_type | solution.py:76
  164.6 3.7 %copy.207 = bf16[256,8,4,16]{3,1,2,0:T(8,128)(2,1)} copy(bf16[256,8,4,16]{0,3,2,1:T(8,128)(2,1)S(1)} %bitcast.240) | data formatting | bytes 524288 | tf_op jit(solution)/shard_map/while/body/eval_jaxpr/reshape | solution.py:65
  168.3 4.1 %convert_bitcast_fusion.2 = bf16[256,8,4,16]{3,1,2,0:T(8,128)(2,1)} fusion(bf16[256,8,4,16]{3,1,2,0:T(8,128)(2,1)} %copy.207, bf16[256,4,8,8]{3,2,1,0:T(8,128)(2,1)S(1)} %copy-done), kind=kOutput, calls=%fused_computation.clone.1 | convolution fusion | flops 2228224 | bytes 655360 | tf_op jit(solution)/shard_map/while/body/eval_jaxpr/phmn,pnhd->pmhd/dot_general | solution.py:77
  172.4 2.7 %copy.212 = bf16[256,8,4,16]{0,3,2,1:T(8,128)(2,1)S(1)} copy(bf16[256,8,4,16]{3,1,2,0:T(8,128)(2,1)} %convert_bitcast_fusion.2) | data formatting | bytes 524288 | tf_op jit(solution)/shard_map/while/body/eval_jaxpr/convert_element_type | solution.py:78
  175.8 2.9 %collective-permute-start.2 = (bf16[8,8,8,4]{3,1,2,0:T(8,128)(2,1)S(1)}, bf16[8,8,8,4]{3,1,2,0:T(8,128)(2,1)S(1)}, u32[]{:S(2)}, u32[]{:S(2)}) collective-permute-start(bf16[8,8,8,4]{3,1,2,0:T(8,128)(2,1)S(1)} %get-tuple-element.127), channel_id=1, source_target_pairs={{0,8},{8,16},{16,24},{1,9},{9,17},{17,25},{2,10},{10,18},{18,26},{... | collective-permute-start | bytes 12296 | tf_op jit(solution)/shard_map/ppermute | solution.py:15
  178.8 1.9 collective-permute-start.3
  180.9 4.2 %collective-permute-done.3 = bf16[8,8,8,4]{3,1,2,0:T(8,128)(2,1)S(1)} collective-permute-done((bf16[8,8,8,4]{3,1,2,0:T(8,128)(2,1)S(1)}, bf16[8,8,8,4]{3,1,2,0:T(8,128)(2,1)S(1)}, u32[]{:S(2)}, u32[]{:S(2)}) %collective-permute-start.3) | collective-permute-done | bytes 4128 | tf_op jit(solution)/shard_map/ppermute | solution.py:18
  185.3 4.1 %collective-permute-start.4 = (bf16[8,8,4,136]{3,1,2,0:T(8,128)(2,1)S(1)}, bf16[8,8,4,136]{3,1,2,0:T(8,128)(2,1)S(1)}, u32[]{:S(2)}, u32[]{:S(2)}) collective-permute-start(bf16[8,8,4,136]{3,1,2,0:T(8,128)(2,1)S(1)} %get-tuple-element.123), channel_id=1, source_target_pairs={{0,1},{1,2},{2,3},{3,4},{4,5},{5,6},{6,7},{8,9},{9,10},{10,11},{11... | collective-permute-start | bytes 208904 | tf_op jit(solution)/shard_map/ppermute | solution.py:15
  189.4 1.5 collective-permute-start.5
  191.3 4.5 %collective-permute-done.5 = bf16[8,8,4,136]{3,1,2,0:T(8,128)(2,1)S(1)} collective-permute-done((bf16[8,8,4,136]{3,1,2,0:T(8,128)(2,1)S(1)}, bf16[8,8,4,136]{3,1,2,0:T(8,128)(2,1)S(1)}, u32[]{:S(2)}, u32[]{:S(2)}) %collective-permute-start.5) | collective-permute-done | bytes 69664 | tf_op jit(solution)/shard_map/ppermute | solution.py:18
  197.9 2.9 %collective-permute-start.6 = (bf16[8,8,8,4]{3,1,2,0:T(8,128)(2,1)S(1)}, bf16[8,8,8,4]{3,1,2,0:T(8,128)(2,1)S(1)}, u32[]{:S(2)}, u32[]{:S(2)}) collective-permute-start(bf16[8,8,8,4]{3,1,2,0:T(8,128)(2,1)S(1)} %get-tuple-element.125), channel_id=1, source_target_pairs={{0,8},{8,16},{16,24},{1,9},{9,17},{17,25},{2,10},{10,18},{18,26},{... | collective-permute-start | bytes 12296 | tf_op jit(solution)/shard_map/ppermute | solution.py:15
  200.8 1.9 collective-permute-start.7
  202.9 4.2 %collective-permute-done.7 = bf16[8,8,8,4]{3,1,2,0:T(8,128)(2,1)S(1)} collective-permute-done((bf16[8,8,8,4]{3,1,2,0:T(8,128)(2,1)S(1)}, bf16[8,8,8,4]{3,1,2,0:T(8,128)(2,1)S(1)}, u32[]{:S(2)}, u32[]{:S(2)}) %collective-permute-start.7) | collective-permute-done | bytes 4128 | tf_op jit(solution)/shard_map/ppermute | solution.py:18
  207.3 4.5 %collective-permute-start.8 = (bf16[8,8,4,136]{3,1,2,0:T(8,128)(2,1)S(1)}, bf16[8,8,4,136]{3,1,2,0:T(8,128)(2,1)S(1)}, u32[]{:S(2)}, u32[]{:S(2)}) collective-permute-start(bf16[8,8,4,136]{3,1,2,0:T(8,128)(2,1)S(1)} %get-tuple-element.121), channel_id=1, source_target_pairs={{0,1},{1,2},{2,3},{3,4},{4,5},{5,6},{6,7},{8,9},{9,10},{10,11},{11... | collective-permute-start | bytes 208904 | tf_op jit(solution)/shard_map/ppermute | solution.py:15
  211.9 1.3 collective-permute-start.9
  213.4 1.8 collective-permute-done.8
  215.1 2.4 %collective-permute-done.9 = bf16[8,8,4,136]{3,1,2,0:T(8,128)(2,1)S(1)} collective-permute-done((bf16[8,8,4,136]{3,1,2,0:T(8,128)(2,1)S(1)}, bf16[8,8,4,136]{3,1,2,0:T(8,128)(2,1)S(1)}, u32[]{:S(2)}, u32[]{:S(2)}) %collective-permute-start.9) | collective-permute-done | bytes 69664 | tf_op jit(solution)/shard_map/ppermute | solution.py:18
  219.5 0.7 copy.154
  (137 shorter events, 16.9 us)
Async XLA Ops:
  0.0 8.7 %copy-start.1 = (bf16[9,8,8]{0,2,1:T(8,128)(2,1)S(1)}, bf16[9,8,8]{0,2,1:T(8,128)(2,1)}, u32[]{:S(2)}) copy-start(bf16[9,8,8]{0,2,1:T(8,128)(2,1)} %param.24) | copy-start | bytes 3460
  3.4 17.3 %collective-permute-start = (f32[5,8,4,512]{3,1,2,0:T(8,128)S(1)}, f32[5,8,4,512]{3,1,2,0:T(8,128)S(1)}, u32[]{:S(2)}, u32[]{:S(2)}) collective-permute-start(f32[5,8,4,512]{3,1,2,0:T(8,128)S(1)} %get-tuple-element.115), channel_id=1, source_target_pairs={{0,1},{1,2},{2,3},{3,4},{4,5},{5,6},{6,7},{8,9},{9,10},{10,11},{11... | collective-permute-start | bytes 983048 | tf_op jit(solution)/shard_map/ppermute | solution.py:15
  7.3 13.4 %collective-permute-start.1 = (f32[5,8,4,512]{3,1,2,0:T(8,128)S(1)}, f32[5,8,4,512]{3,1,2,0:T(8,128)S(1)}, u32[]{:S(2)}, u32[]{:S(2)}) collective-permute-start(f32[5,8,4,512]{3,1,2,0:T(8,128)S(1)} %get-tuple-element.116), channel_id=1, source_target_pairs={{1,0},{2,1},{3,2},{4,3},{5,4},{6,5},{7,6},{9,8},{10,9},{11,10},{12... | collective-permute-start | bytes 983048 | tf_op jit(solution)/shard_map/ppermute | solution.py:18
  22.7 9.7 %copy-start.2 = (bf16[9,8,8]{0,2,1:T(8,128)(2,1)S(1)}, bf16[9,8,8]{0,2,1:T(8,128)(2,1)}, u32[]{:S(2)}) copy-start(bf16[9,8,8]{0,2,1:T(8,128)(2,1)} %param.25) | copy-start | bytes 3460
  22.7 9.8 %copy-start.7 = (bf16[64,64]{1,0:T(8,128)(2,1)S(1)}, bf16[64,64]{1,0:T(8,128)(2,1)}, u32[]{:S(2)}) copy-start(bf16[64,64]{1,0:T(8,128)(2,1)} %param.22) | copy-start | bytes 24580
  27.6 8.4 %all-to-all-start = ((bf16[4,2,8192]{2,1,0:T(2,128)(2,1)}), bf16[4,2,8192]{2,1,0:T(2,128)(2,1)S(1)}, u32[]{:S(2)}, u32[]{:S(2)}) async-start(bf16[4,2,8192]{2,1,0:T(2,128)(2,1)} %reshape.99), calls=%async_computation | async-start | bytes 262144 | tf_op jit(solution)/shard_map/all_to_all | solution.py:142
  35.0 5.1 %copy-start.3 = (bf16[64,192]{1,0:T(8,128)(2,1)S(1)}, bf16[64,192]{1,0:T(8,128)(2,1)}, u32[]{:S(2)}) copy-start(bf16[64,192]{1,0:T(8,128)(2,1)} %param.20) | copy-start | bytes 73732
  35.1 5.1 %copy-start.4 = (bf16[64,8]{0,1:T(8,128)(2,1)S(1)}, bf16[64,8]{0,1:T(8,128)(2,1)}, u32[]{:S(2)}) copy-start(bf16[64,8]{0,1:T(8,128)(2,1)} %param.23) | copy-start | bytes 3076
  35.1 5.1 %copy-start.5 = (f32[4]{0:T(128)S(1)}, f32[4]{0:T(128)}, u32[]{:S(2)}) copy-start(f32[4]{0:T(128)} %param.21) | copy-start | bytes 52
  35.1 5.1 %copy-start.6 = (bf16[8,64]{1,0:T(8,128)(2,1)S(1)}, bf16[8,64]{1,0:T(8,128)(2,1)}, u32[]{:S(2)}) copy-start(bf16[8,64]{1,0:T(8,128)(2,1)} %param.18) | copy-start | bytes 3076
  35.1 5.1 %copy-start.8 = (f32[64]{0:T(128)S(1)}, f32[64]{0:T(128)}, u32[]{:S(2)}) copy-start(f32[64]{0:T(128)} %param.19) | copy-start | bytes 772
  63.2 3.7 %copy-start = (bf16[256,4,8,8]{3,2,1,0:T(8,128)(2,1)S(1)}, bf16[256,4,8,8]{3,2,1,0:T(8,128)(2,1)}, u32[]{:S(2)}) copy-start(bf16[256,4,8,8]{3,2,1,0:T(8,128)(2,1)} %copy.211) | copy-start | bytes 393220 | tf_op jit(solution)/shard_map/while
  97.0 3.7 %copy-start = (bf16[256,4,8,8]{3,2,1,0:T(8,128)(2,1)S(1)}, bf16[256,4,8,8]{3,2,1,0:T(8,128)(2,1)}, u32[]{:S(2)}) copy-start(bf16[256,4,8,8]{3,2,1,0:T(8,128)(2,1)} %copy.211) | copy-start | bytes 393220 | tf_op jit(solution)/shard_map/while
  130.8 3.7 %copy-start = (bf16[256,4,8,8]{3,2,1,0:T(8,128)(2,1)S(1)}, bf16[256,4,8,8]{3,2,1,0:T(8,128)(2,1)}, u32[]{:S(2)}) copy-start(bf16[256,4,8,8]{3,2,1,0:T(8,128)(2,1)} %copy.211) | copy-start | bytes 393220 | tf_op jit(solution)/shard_map/while
  164.6 3.7 %copy-start = (bf16[256,4,8,8]{3,2,1,0:T(8,128)(2,1)S(1)}, bf16[256,4,8,8]{3,2,1,0:T(8,128)(2,1)}, u32[]{:S(2)}) copy-start(bf16[256,4,8,8]{3,2,1,0:T(8,128)(2,1)} %copy.211) | copy-start | bytes 393220 | tf_op jit(solution)/shard_map/while
  175.8 5.0 %collective-permute-start.2 = (bf16[8,8,8,4]{3,1,2,0:T(8,128)(2,1)S(1)}, bf16[8,8,8,4]{3,1,2,0:T(8,128)(2,1)S(1)}, u32[]{:S(2)}, u32[]{:S(2)}) collective-permute-start(bf16[8,8,8,4]{3,1,2,0:T(8,128)(2,1)S(1)} %get-tuple-element.127), channel_id=1, source_target_pairs={{0,8},{8,16},{16,24},{1,9},{9,17},{17,25},{2,10},{10,18},{18,26},{... | collective-permute-start | bytes 12296 | tf_op jit(solution)/shard_map/ppermute | solution.py:15
  178.8 6.3 %collective-permute-start.3 = (bf16[8,8,8,4]{3,1,2,0:T(8,128)(2,1)S(1)}, bf16[8,8,8,4]{3,1,2,0:T(8,128)(2,1)S(1)}, u32[]{:S(2)}, u32[]{:S(2)}) collective-permute-start(bf16[8,8,8,4]{3,1,2,0:T(8,128)(2,1)S(1)} %get-tuple-element.128), channel_id=1, source_target_pairs={{8,0},{16,8},{24,16},{9,1},{17,9},{25,17},{10,2},{18,10},{26,18},{... | collective-permute-start | bytes 12296 | tf_op jit(solution)/shard_map/ppermute | solution.py:18
  185.3 6.0 %collective-permute-start.4 = (bf16[8,8,4,136]{3,1,2,0:T(8,128)(2,1)S(1)}, bf16[8,8,4,136]{3,1,2,0:T(8,128)(2,1)S(1)}, u32[]{:S(2)}, u32[]{:S(2)}) collective-permute-start(bf16[8,8,4,136]{3,1,2,0:T(8,128)(2,1)S(1)} %get-tuple-element.123), channel_id=1, source_target_pairs={{0,1},{1,2},{2,3},{3,4},{4,5},{5,6},{6,7},{8,9},{9,10},{10,11},{11... | collective-permute-start | bytes 208904 | tf_op jit(solution)/shard_map/ppermute | solution.py:15
  189.4 6.4 %collective-permute-start.5 = (bf16[8,8,4,136]{3,1,2,0:T(8,128)(2,1)S(1)}, bf16[8,8,4,136]{3,1,2,0:T(8,128)(2,1)S(1)}, u32[]{:S(2)}, u32[]{:S(2)}) collective-permute-start(bf16[8,8,4,136]{3,1,2,0:T(8,128)(2,1)S(1)} %get-tuple-element.124), channel_id=1, source_target_pairs={{1,0},{2,1},{3,2},{4,3},{5,4},{6,5},{7,6},{9,8},{10,9},{11,10},{12... | collective-permute-start | bytes 208904 | tf_op jit(solution)/shard_map/ppermute | solution.py:18
  197.9 5.0 %collective-permute-start.6 = (bf16[8,8,8,4]{3,1,2,0:T(8,128)(2,1)S(1)}, bf16[8,8,8,4]{3,1,2,0:T(8,128)(2,1)S(1)}, u32[]{:S(2)}, u32[]{:S(2)}) collective-permute-start(bf16[8,8,8,4]{3,1,2,0:T(8,128)(2,1)S(1)} %get-tuple-element.125), channel_id=1, source_target_pairs={{0,8},{8,16},{16,24},{1,9},{9,17},{17,25},{2,10},{10,18},{18,26},{... | collective-permute-start | bytes 12296 | tf_op jit(solution)/shard_map/ppermute | solution.py:15
  200.8 6.3 %collective-permute-start.7 = (bf16[8,8,8,4]{3,1,2,0:T(8,128)(2,1)S(1)}, bf16[8,8,8,4]{3,1,2,0:T(8,128)(2,1)S(1)}, u32[]{:S(2)}, u32[]{:S(2)}) collective-permute-start(bf16[8,8,8,4]{3,1,2,0:T(8,128)(2,1)S(1)} %get-tuple-element.126), channel_id=1, source_target_pairs={{8,0},{16,8},{24,16},{9,1},{17,9},{25,17},{10,2},{18,10},{26,18},{... | collective-permute-start | bytes 12296 | tf_op jit(solution)/shard_map/ppermute | solution.py:18
  207.3 7.8 %collective-permute-start.8 = (bf16[8,8,4,136]{3,1,2,0:T(8,128)(2,1)S(1)}, bf16[8,8,4,136]{3,1,2,0:T(8,128)(2,1)S(1)}, u32[]{:S(2)}, u32[]{:S(2)}) collective-permute-start(bf16[8,8,4,136]{3,1,2,0:T(8,128)(2,1)S(1)} %get-tuple-element.121), channel_id=1, source_target_pairs={{0,1},{1,2},{2,3},{3,4},{4,5},{5,6},{6,7},{8,9},{9,10},{10,11},{11... | collective-permute-start | bytes 208904 | tf_op jit(solution)/shard_map/ppermute | solution.py:15
  211.9 5.7 %collective-permute-start.9 = (bf16[8,8,4,136]{3,1,2,0:T(8,128)(2,1)S(1)}, bf16[8,8,4,136]{3,1,2,0:T(8,128)(2,1)S(1)}, u32[]{:S(2)}, u32[]{:S(2)}) collective-permute-start(bf16[8,8,4,136]{3,1,2,0:T(8,128)(2,1)S(1)} %get-tuple-element.122), channel_id=1, source_target_pairs={{1,0},{2,1},{3,2},{4,3},{5,4},{6,5},{7,6},{9,8},{10,9},{11,10},{12... | collective-permute-start | bytes 208904 | tf_op jit(solution)/shard_map/ppermute | solution.py:18
where the time goes:
time: 221 us; the launch traced here: 220 us
  local copies, waits for them, and re-layouts  104 us (47%)
  matrix products  46 us (21%)
  starting transfers between devices  31.2 us (14%)
  waiting for transfers between devices  30 us (14%)
  other arithmetic  5.64 us (3%)
  loops' own time  3.16 us (1%)
    dot_general x4, matrix products, post_block(): jnp.einsum('pmhd,pnhd->phmn', queries, keys_all, preferred_element_type=j...  21.6 us
    ppermute x5, starting transfers between devices, padded(): lax.ppermute(lax.slice_in_dim(block, block.shape[dim] - width, None, axis...  18.5 us
    dot_general x4, matrix products, post_block(): jnp.einsum('phmn,pnhd->pmhd', probs, values, preferred_element_type=jnp.f...  16.5 us
    ppermute x5, waiting for transfers between devices, padded(): lax.ppermute(lax.slice_in_dim(block, 0, width, axis=dim), axis, backward)  15.3 us
    convert_element_type x4, local copies, waits for them, and re-layouts, post_block(): (keys_all * lax.rsqrt(jnp.sum(keys_all * keys_all, -1, keepdims=True) + 1...  15.2 us
    convert_element_type x4, local copies, waits for them, and re-layouts, post_block(): (queries * lax.rsqrt(jnp.sum(queries * queries, -1, keepdims=True) + 1.0)...  14.9 us
    reshape x4, local copies, waits for them, and re-layouts, post_block(): projected[..., 2 * width:].astype(jnp.bfloat16)  14.8 us
    convert_element_type x4, local copies, waits for them, and re-layouts, post_block(): probs = (weights / jnp.sum(weights, -1, keepdims=True)).astype(jnp.bfloat16)  14.6 us
  transfers between devices with their start and end apart: 11, of which 8 were waited for; matrix products, arithmetic and copies ran while one was open for 2% of the time, Pallas kernels for 0%

commit v1 on v0

--- a/solution.py
+++ b/solution.py
@@ -139,8 +139,11 @@
         inside = (row_ids >= 0) & (row_ids < all_rows)
         gridded_quantity_list = jnp.where(inside[None, None, :, None], gridded_quantity_list, 0.0)
     predicted_states = gridded_quantity_list.astype(jnp.bfloat16)
-    blockwise_quantity = lax.all_to_all(
-        predicted_states, "mem", split_axis=3, concat_axis=0, tiled=True
+    blockwise_quantity = jnp.concatenate(
+        lax.all_to_all(
+            jnp.stack(jnp.split(predicted_states, lax.axis_size("mem"), axis=3)), "mem", 0, 0
+        ),
+        axis=0,
     )
     members, levels_count, tile_rows, tile_cols = blockwise_quantity.shape
     count = tile_rows * tile_cols

time: 221 us -> 213 us (0.964)
  local copies, waits for them, and re-layouts: 104 us -> 94.7 us
    unnamed x39 -> x37, local copies, waits for them, and re-layouts: 11 us -> 5.7 us
where the time goes in v1:
time: 213 us; the launch traced here: 212 us
  local copies, waits for them, and re-layouts  94.7 us (44%)
  matrix products  46.1 us (22%)
  starting transfers between devices  31.2 us (15%)
  waiting for transfers between devices  30 us (14%)
  other arithmetic  6.32 us (3%)
  loops' own time  2.98 us (1%)
    dot_general x4, matrix products, post_block(): jnp.einsum('pmhd,pnhd->phmn', queries, keys_all, preferred_element_type=j...  21.6 us
    ppermute x5, starting transfers between devices, padded(): lax.ppermute(lax.slice_in_dim(block, block.shape[dim] - width, None, axis...  18.5 us
    dot_general x4, matrix products, post_block(): jnp.einsum('phmn,pnhd->pmhd', probs, values, preferred_element_type=jnp.f...  16.5 us
    ppermute x5, waiting for transfers between devices, padded(): lax.ppermute(lax.slice_in_dim(block, 0, width, axis=dim), axis, backward)  15.3 us
    convert_element_type x4, local copies, waits for them, and re-layouts, post_block(): (keys_all * lax.rsqrt(jnp.sum(keys_all * keys_all, -1, keepdims=True) + 1...  15.3 us
    convert_element_type x4, local copies, waits for them, and re-layouts, post_block(): (queries * lax.rsqrt(jnp.sum(queries * queries, -1, keepdims=True) + 1.0)...  14.9 us
    reshape x4, local copies, waits for them, and re-layouts, post_block(): projected[..., 2 * width:].astype(jnp.bfloat16)  14.8 us
    convert_element_type x4, local copies, waits for them, and re-layouts, post_block(): probs = (weights / jnp.sum(weights, -1, keepdims=True)).astype(jnp.bfloat16)  14.6 us
  transfers between devices with their start and end apart: 11, of which 8 were waited for; matrix products, arithmetic and copies ran while one was open for 2% of the time, Pallas kernels for 0%

profile of v1, /device:TPU:1, one launch (start us, length us, event | category | flops | bytes accessed | tf_op | source)
XLA Modules:
  0.0 211.9 jit_solution(11141641986793755540)
XLA Ops:
  0.0 1.0 copy.194
  1.0 1.1 copy.117
  2.1 1.1 fusion.90
  3.4 4.0 %collective-permute-start = (f32[5,8,4,512]{3,1,2,0:T(8,128)S(1)}, f32[5,8,4,512]{3,1,2,0:T(8,128)S(1)}, u32[]{:S(2)}, u32[]{:S(2)}) collective-permute-start(f32[5,8,4,512]{3,1,2,0:T(8,128)S(1)} %get-tuple-element.115), channel_id=1, source_target_pairs={{0,1},{1,2},{2,3},{3,4},{4,5},{5,6},{6,7},{8,9},{9,10},{10,11},{11... | collective-permute-start | bytes 983048 | tf_op jit(solution)/shard_map/ppermute | solution.py:15
  7.3 1.3 collective-permute-start.1
  8.8 11.9 %collective-permute-done = f32[5,8,4,512]{3,1,2,0:T(8,128)S(1)} collective-permute-done((f32[5,8,4,512]{3,1,2,0:T(8,128)S(1)}, f32[5,8,4,512]{3,1,2,0:T(8,128)S(1)}, u32[]{:S(2)}, u32[]{:S(2)}) %collective-permute-start) | collective-permute-done | bytes 327712 | tf_op jit(solution)/shard_map/ppermute | solution.py:15
  21.0 0.5 add_select_fusion
  21.5 0.4 add_select_fusion.1
  22.8 0.7 pad_maximum_fusion.14
  23.5 4.8 %all-to-all-start = ((bf16[4,2,8,8,128]{4,2,3,1,0:T(8,128)(2,1)}), bf16[4,2,8,8,128]{4,2,3,1,0:T(8,128)(2,1)S(1)}, u32[]{:S(2)}, u32[]{:S(2)}) async-start(bf16[4,2,8,8,128]{4,2,3,1,0:T(8,128)(2,1)} %pad_maximum_fusion.14), calls=%async_computation | async-start | bytes 262144 | tf_op jit(solution)/shard_map/all_to_all | solution.py:143
  31.0 0.9 all-to-all-done
  31.9 135.3 %while.10 = (s32[]{:T(128)}, bf16[4,8,8,256]{3,2,1,0:T(8,128)(2,1)S(1)}, s32[4]{0:T(128)S(1)}, bf16[8,8,1024]{2,1,0:T(8,128)(2,1)S(1)}, bf16[8,64]{1,0:T(8,128)(...) while((s32[]{:T(128)}, ...), condition=%wide.region_5.6_spmd, body=%wide.region_0.5_spmd.sunk | while | flops 77932544 | bytes 12530179 | solution.py:165
  32.0 0.6 dynamic_slice.14
  33.5 0.4 fusion.122
  34.4 3.7 %copy.202 = bf16[256,8,4,16]{3,1,2,0:T(8,128)(2,1)} copy(bf16[256,8,4,16]{0,3,2,1:T(8,128)(2,1)S(1)} %get-tuple-element.234) | data formatting | bytes 524288 | tf_op jit(solution)/shard_map/while/body/eval_jaxpr/convert_element_type | solution.py:67
  38.1 3.8 %copy.203 = bf16[256,8,4,16]{3,1,2,0:T(8,128)(2,1)} copy(bf16[256,8,4,16]{0,3,2,1:T(8,128)(2,1)S(1)} %get-tuple-element.235) | data formatting | bytes 524288 | tf_op jit(solution)/shard_map/while/body/eval_jaxpr/convert_element_type | solution.py:70
  41.9 5.4 %fusion.123 = f32[256,4,8,8]{2,3,1,0:T(8,128)} fusion(bf16[256,8,4,16]{3,1,2,0:T(8,128)(2,1)} %copy.202, bf16[256,8,4,16]{3,1,2,0:T(8,128)(2,1)} %copy.203), kind=kOutput, calls=%fused_computation.159.clone.1 | convolution fusion | flops 2097152 | bytes 786432 | tf_op jit(solution)/shard_map/while/body/eval_jaxpr/pmhd,pnhd->phmn/dot_general | solution.py:73
  47.3 3.6 %copy.204 = f32[256,4,8,8]{0,3,2,1:T(8,128)S(1)} copy(f32[256,4,8,8]{2,3,1,0:T(8,128)} %fusion.123) | data formatting | bytes 524288 | tf_op jit(solution)/shard_map/while/body/eval_jaxpr/pmhd,pnhd->phmn/dot_general | solution.py:73
  51.2 3.7 %copy.205 = bf16[256,4,8,8]{3,2,1,0:T(8,128)(2,1)} copy(bf16[256,4,8,8]{0,3,2,1:T(8,128)(2,1)S(1)} %divide_convert_fusion.2) | data formatting | bytes 262144 | tf_op jit(solution)/shard_map/while/body/eval_jaxpr/convert_element_type | solution.py:76
  54.9 3.7 %copy.201 = bf16[256,8,4,16]{3,1,2,0:T(8,128)(2,1)} copy(bf16[256,8,4,16]{0,3,2,1:T(8,128)(2,1)S(1)} %bitcast.243) | data formatting | bytes 524288 | tf_op jit(solution)/shard_map/while/body/eval_jaxpr/reshape | solution.py:65
  58.6 4.1 %convert_bitcast_fusion.2 = bf16[256,8,4,16]{3,1,2,0:T(8,128)(2,1)} fusion(bf16[256,8,4,16]{3,1,2,0:T(8,128)(2,1)} %copy.201, bf16[256,4,8,8]{3,2,1,0:T(8,128)(2,1)S(1)} %copy-done), kind=kOutput, calls=%fused_computation.clone.1 | convolution fusion | flops 2228224 | bytes 655360 | tf_op jit(solution)/shard_map/while/body/eval_jaxpr/phmn,pnhd->pmhd/dot_general | solution.py:77
  62.7 2.7 %copy.206 = bf16[256,8,4,16]{0,3,2,1:T(8,128)(2,1)S(1)} copy(bf16[256,8,4,16]{3,1,2,0:T(8,128)(2,1)} %convert_bitcast_fusion.2) | data formatting | bytes 524288 | tf_op jit(solution)/shard_map/while/body/eval_jaxpr/convert_element_type | solution.py:78
  65.8 0.6 dynamic_slice.14
  68.2 3.7 %copy.202 = bf16[256,8,4,16]{3,1,2,0:T(8,128)(2,1)} copy(bf16[256,8,4,16]{0,3,2,1:T(8,128)(2,1)S(1)} %get-tuple-element.234) | data formatting | bytes 524288 | tf_op jit(solution)/shard_map/while/body/eval_jaxpr/convert_element_type | solution.py:67
  71.9 3.8 %copy.203 = bf16[256,8,4,16]{3,1,2,0:T(8,128)(2,1)} copy(bf16[256,8,4,16]{0,3,2,1:T(8,128)(2,1)S(1)} %get-tuple-element.235) | data formatting | bytes 524288 | tf_op jit(solution)/shard_map/while/body/eval_jaxpr/convert_element_type | solution.py:70
  75.7 5.4 %fusion.123 = f32[256,4,8,8]{2,3,1,0:T(8,128)} fusion(bf16[256,8,4,16]{3,1,2,0:T(8,128)(2,1)} %copy.202, bf16[256,8,4,16]{3,1,2,0:T(8,128)(2,1)} %copy.203), kind=kOutput, calls=%fused_computation.159.clone.1 | convolution fusion | flops 2097152 | bytes 786432 | tf_op jit(solution)/shard_map/while/body/eval_jaxpr/pmhd,pnhd->phmn/dot_general | solution.py:73
  81.1 3.6 %copy.204 = f32[256,4,8,8]{0,3,2,1:T(8,128)S(1)} copy(f32[256,4,8,8]{2,3,1,0:T(8,128)} %fusion.123) | data formatting | bytes 524288 | tf_op jit(solution)/shard_map/while/body/eval_jaxpr/pmhd,pnhd->phmn/dot_general | solution.py:73
  85.0 3.7 %copy.205 = bf16[256,4,8,8]{3,2,1,0:T(8,128)(2,1)} copy(bf16[256,4,8,8]{0,3,2,1:T(8,128)(2,1)S(1)} %divide_convert_fusion.2) | data formatting | bytes 262144 | tf_op jit(solution)/shard_map/while/body/eval_jaxpr/convert_element_type | solution.py:76
  88.7 3.7 %copy.201 = bf16[256,8,4,16]{3,1,2,0:T(8,128)(2,1)} copy(bf16[256,8,4,16]{0,3,2,1:T(8,128)(2,1)S(1)} %bitcast.243) | data formatting | bytes 524288 | tf_op jit(solution)/shard_map/while/body/eval_jaxpr/reshape | solution.py:65
  92.4 4.1 %convert_bitcast_fusion.2 = bf16[256,8,4,16]{3,1,2,0:T(8,128)(2,1)} fusion(bf16[256,8,4,16]{3,1,2,0:T(8,128)(2,1)} %copy.201, bf16[256,4,8,8]{3,2,1,0:T(8,128)(2,1)S(1)} %copy-done), kind=kOutput, calls=%fused_computation.clone.1 | convolution fusion | flops 2228224 | bytes 655360 | tf_op jit(solution)/shard_map/while/body/eval_jaxpr/phmn,pnhd->pmhd/dot_general | solution.py:77
  96.5 2.7 %copy.206 = bf16[256,8,4,16]{0,3,2,1:T(8,128)(2,1)S(1)} copy(bf16[256,8,4,16]{3,1,2,0:T(8,128)(2,1)} %convert_bitcast_fusion.2) | data formatting | bytes 524288 | tf_op jit(solution)/shard_map/while/body/eval_jaxpr/convert_element_type | solution.py:78
  99.6 0.6 dynamic_slice.14
  101.2 0.4 fusion.122
  102.0 3.7 %copy.202 = bf16[256,8,4,16]{3,1,2,0:T(8,128)(2,1)} copy(bf16[256,8,4,16]{0,3,2,1:T(8,128)(2,1)S(1)} %get-tuple-element.234) | data formatting | bytes 524288 | tf_op jit(solution)/shard_map/while/body/eval_jaxpr/convert_element_type | solution.py:67
  105.8 3.8 %copy.203 = bf16[256,8,4,16]{3,1,2,0:T(8,128)(2,1)} copy(bf16[256,8,4,16]{0,3,2,1:T(8,128)(2,1)S(1)} %get-tuple-element.235) | data formatting | bytes 524288 | tf_op jit(solution)/shard_map/while/body/eval_jaxpr/convert_element_type | solution.py:70
  109.6 5.4 %fusion.123 = f32[256,4,8,8]{2,3,1,0:T(8,128)} fusion(bf16[256,8,4,16]{3,1,2,0:T(8,128)(2,1)} %copy.202, bf16[256,8,4,16]{3,1,2,0:T(8,128)(2,1)} %copy.203), kind=kOutput, calls=%fused_computation.159.clone.1 | convolution fusion | flops 2097152 | bytes 786432 | tf_op jit(solution)/shard_map/while/body/eval_jaxpr/pmhd,pnhd->phmn/dot_general | solution.py:73
  115.0 3.6 %copy.204 = f32[256,4,8,8]{0,3,2,1:T(8,128)S(1)} copy(f32[256,4,8,8]{2,3,1,0:T(8,128)} %fusion.123) | data formatting | bytes 524288 | tf_op jit(solution)/shard_map/while/body/eval_jaxpr/pmhd,pnhd->phmn/dot_general | solution.py:73
  118.8 3.7 %copy.205 = bf16[256,4,8,8]{3,2,1,0:T(8,128)(2,1)} copy(bf16[256,4,8,8]{0,3,2,1:T(8,128)(2,1)S(1)} %divide_convert_fusion.2) | data formatting | bytes 262144 | tf_op jit(solution)/shard_map/while/body/eval_jaxpr/convert_element_type | solution.py:76
  122.5 3.7 %copy.201 = bf16[256,8,4,16]{3,1,2,0:T(8,128)(2,1)} copy(bf16[256,8,4,16]{0,3,2,1:T(8,128)(2,1)S(1)} %bitcast.243) | data formatting | bytes 524288 | tf_op jit(solution)/shard_map/while/body/eval_jaxpr/reshape | solution.py:65
  126.2 4.1 %convert_bitcast_fusion.2 = bf16[256,8,4,16]{3,1,2,0:T(8,128)(2,1)} fusion(bf16[256,8,4,16]{3,1,2,0:T(8,128)(2,1)} %copy.201, bf16[256,4,8,8]{3,2,1,0:T(8,128)(2,1)S(1)} %copy-done), kind=kOutput, calls=%fused_computation.clone.1 | convolution fusion | flops 2228224 | bytes 655360 | tf_op jit(solution)/shard_map/while/body/eval_jaxpr/phmn,pnhd->pmhd/dot_general | solution.py:77
  130.4 2.7 %copy.206 = bf16[256,8,4,16]{0,3,2,1:T(8,128)(2,1)S(1)} copy(bf16[256,8,4,16]{3,1,2,0:T(8,128)(2,1)} %convert_bitcast_fusion.2) | data formatting | bytes 524288 | tf_op jit(solution)/shard_map/while/body/eval_jaxpr/convert_element_type | solution.py:78
  133.5 0.6 dynamic_slice.14
  135.9 3.7 %copy.202 = bf16[256,8,4,16]{3,1,2,0:T(8,128)(2,1)} copy(bf16[256,8,4,16]{0,3,2,1:T(8,128)(2,1)S(1)} %get-tuple-element.234) | data formatting | bytes 524288 | tf_op jit(solution)/shard_map/while/body/eval_jaxpr/convert_element_type | solution.py:67
  139.6 3.8 %copy.203 = bf16[256,8,4,16]{3,1,2,0:T(8,128)(2,1)} copy(bf16[256,8,4,16]{0,3,2,1:T(8,128)(2,1)S(1)} %get-tuple-element.235) | data formatting | bytes 524288 | tf_op jit(solution)/shard_map/while/body/eval_jaxpr/convert_element_type | solution.py:70
  143.4 5.4 %fusion.123 = f32[256,4,8,8]{2,3,1,0:T(8,128)} fusion(bf16[256,8,4,16]{3,1,2,0:T(8,128)(2,1)} %copy.202, bf16[256,8,4,16]{3,1,2,0:T(8,128)(2,1)} %copy.203), kind=kOutput, calls=%fused_computation.159.clone.1 | convolution fusion | flops 2097152 | bytes 786432 | tf_op jit(solution)/shard_map/while/body/eval_jaxpr/pmhd,pnhd->phmn/dot_general | solution.py:73
  148.8 3.6 %copy.204 = f32[256,4,8,8]{0,3,2,1:T(8,128)S(1)} copy(f32[256,4,8,8]{2,3,1,0:T(8,128)} %fusion.123) | data formatting | bytes 524288 | tf_op jit(solution)/shard_map/while/body/eval_jaxpr/pmhd,pnhd->phmn/dot_general | solution.py:73
  152.7 3.7 %copy.205 = bf16[256,4,8,8]{3,2,1,0:T(8,128)(2,1)} copy(bf16[256,4,8,8]{0,3,2,1:T(8,128)(2,1)S(1)} %divide_convert_fusion.2) | data formatting | bytes 262144 | tf_op jit(solution)/shard_map/while/body/eval_jaxpr/convert_element_type | solution.py:76
  156.4 3.7 %copy.201 = bf16[256,8,4,16]{3,1,2,0:T(8,128)(2,1)} copy(bf16[256,8,4,16]{0,3,2,1:T(8,128)(2,1)S(1)} %bitcast.243) | data formatting | bytes 524288 | tf_op jit(solution)/shard_map/while/body/eval_jaxpr/reshape | solution.py:65
  160.1 4.1 %convert_bitcast_fusion.2 = bf16[256,8,4,16]{3,1,2,0:T(8,128)(2,1)} fusion(bf16[256,8,4,16]{3,1,2,0:T(8,128)(2,1)} %copy.201, bf16[256,4,8,8]{3,2,1,0:T(8,128)(2,1)S(1)} %copy-done), kind=kOutput, calls=%fused_computation.clone.1 | convolution fusion | flops 2228224 | bytes 655360 | tf_op jit(solution)/shard_map/while/body/eval_jaxpr/phmn,pnhd->pmhd/dot_general | solution.py:77
  164.2 2.7 %copy.206 = bf16[256,8,4,16]{0,3,2,1:T(8,128)(2,1)S(1)} copy(bf16[256,8,4,16]{3,1,2,0:T(8,128)(2,1)} %convert_bitcast_fusion.2) | data formatting | bytes 524288 | tf_op jit(solution)/shard_map/while/body/eval_jaxpr/convert_element_type | solution.py:78
  167.6 2.9 %collective-permute-start.2 = (bf16[8,8,8,4]{3,1,2,0:T(8,128)(2,1)S(1)}, bf16[8,8,8,4]{3,1,2,0:T(8,128)(2,1)S(1)}, u32[]{:S(2)}, u32[]{:S(2)}) collective-permute-start(bf16[8,8,8,4]{3,1,2,0:T(8,128)(2,1)S(1)} %get-tuple-element.127), channel_id=1, source_target_pairs={{0,8},{8,16},{16,24},{1,9},{9,17},{17,25},{2,10},{10,18},{18,26},{... | collective-permute-start | bytes 12296 | tf_op jit(solution)/shard_map/ppermute | solution.py:15
  170.5 1.9 collective-permute-start.3
  172.6 4.2 %collective-permute-done.3 = bf16[8,8,8,4]{3,1,2,0:T(8,128)(2,1)S(1)} collective-permute-done((bf16[8,8,8,4]{3,1,2,0:T(8,128)(2,1)S(1)}, bf16[8,8,8,4]{3,1,2,0:T(8,128)(2,1)S(1)}, u32[]{:S(2)}, u32[]{:S(2)}) %collective-permute-start.3) | collective-permute-done | bytes 4128 | tf_op jit(solution)/shard_map/ppermute | solution.py:18
  177.0 4.1 %collective-permute-start.4 = (bf16[8,8,4,136]{3,1,2,0:T(8,128)(2,1)S(1)}, bf16[8,8,4,136]{3,1,2,0:T(8,128)(2,1)S(1)}, u32[]{:S(2)}, u32[]{:S(2)}) collective-permute-start(bf16[8,8,4,136]{3,1,2,0:T(8,128)(2,1)S(1)} %get-tuple-element.123), channel_id=1, source_target_pairs={{0,1},{1,2},{2,3},{3,4},{4,5},{5,6},{6,7},{8,9},{9,10},{10,11},{11... | collective-permute-start | bytes 208904 | tf_op jit(solution)/shard_map/ppermute | solution.py:15
  181.1 1.5 collective-permute-start.5
  183.1 4.5 %collective-permute-done.5 = bf16[8,8,4,136]{3,1,2,0:T(8,128)(2,1)S(1)} collective-permute-done((bf16[8,8,4,136]{3,1,2,0:T(8,128)(2,1)S(1)}, bf16[8,8,4,136]{3,1,2,0:T(8,128)(2,1)S(1)}, u32[]{:S(2)}, u32[]{:S(2)}) %collective-permute-start.5) | collective-permute-done | bytes 69664 | tf_op jit(solution)/shard_map/ppermute | solution.py:18
  189.6 2.9 %collective-permute-start.6 = (bf16[8,8,8,4]{3,1,2,0:T(8,128)(2,1)S(1)}, bf16[8,8,8,4]{3,1,2,0:T(8,128)(2,1)S(1)}, u32[]{:S(2)}, u32[]{:S(2)}) collective-permute-start(bf16[8,8,8,4]{3,1,2,0:T(8,128)(2,1)S(1)} %get-tuple-element.125), channel_id=1, source_target_pairs={{0,8},{8,16},{16,24},{1,9},{9,17},{17,25},{2,10},{10,18},{18,26},{... | collective-permute-start | bytes 12296 | tf_op jit(solution)/shard_map/ppermute | solution.py:15
  192.6 1.9 collective-permute-start.7
  194.7 4.2 %collective-permute-done.7 = bf16[8,8,8,4]{3,1,2,0:T(8,128)(2,1)S(1)} collective-permute-done((bf16[8,8,8,4]{3,1,2,0:T(8,128)(2,1)S(1)}, bf16[8,8,8,4]{3,1,2,0:T(8,128)(2,1)S(1)}, u32[]{:S(2)}, u32[]{:S(2)}) %collective-permute-start.7) | collective-permute-done | bytes 4128 | tf_op jit(solution)/shard_map/ppermute | solution.py:18
  199.1 4.5 %collective-permute-start.8 = (bf16[8,8,4,136]{3,1,2,0:T(8,128)(2,1)S(1)}, bf16[8,8,4,136]{3,1,2,0:T(8,128)(2,1)S(1)}, u32[]{:S(2)}, u32[]{:S(2)}) collective-permute-start(bf16[8,8,4,136]{3,1,2,0:T(8,128)(2,1)S(1)} %get-tuple-element.121), channel_id=1, source_target_pairs={{0,1},{1,2},{2,3},{3,4},{4,5},{5,6},{6,7},{8,9},{9,10},{10,11},{11... | collective-permute-start | bytes 208904 | tf_op jit(solution)/shard_map/ppermute | solution.py:15
  203.6 1.3 collective-permute-start.9
  205.1 1.8 collective-permute-done.8
  206.9 2.4 %collective-permute-done.9 = bf16[8,8,4,136]{3,1,2,0:T(8,128)(2,1)S(1)} collective-permute-done((bf16[8,8,4,136]{3,1,2,0:T(8,128)(2,1)S(1)}, bf16[8,8,4,136]{3,1,2,0:T(8,128)(2,1)S(1)}, u32[]{:S(2)}, u32[]{:S(2)}) %collective-permute-start.9) | collective-permute-done | bytes 69664 | tf_op jit(solution)/shard_map/ppermute | solution.py:18
  211.2 0.7 copy.148
  (135 shorter events, 15.7 us)
Async XLA Ops:
  0.0 8.7 %copy-start.1 = (bf16[9,8,8]{0,2,1:T(8,128)(2,1)S(1)}, bf16[9,8,8]{0,2,1:T(8,128)(2,1)}, u32[]{:S(2)}) copy-start(bf16[9,8,8]{0,2,1:T(8,128)(2,1)} %param.24) | copy-start | bytes 3460
  3.4 17.3 %collective-permute-start = (f32[5,8,4,512]{3,1,2,0:T(8,128)S(1)}, f32[5,8,4,512]{3,1,2,0:T(8,128)S(1)}, u32[]{:S(2)}, u32[]{:S(2)}) collective-permute-start(f32[5,8,4,512]{3,1,2,0:T(8,128)S(1)} %get-tuple-element.115), channel_id=1, source_target_pairs={{0,1},{1,2},{2,3},{3,4},{4,5},{5,6},{6,7},{8,9},{9,10},{10,11},{11... | collective-permute-start | bytes 983048 | tf_op jit(solution)/shard_map/ppermute | solution.py:15
  7.3 13.4 %collective-permute-start.1 = (f32[5,8,4,512]{3,1,2,0:T(8,128)S(1)}, f32[5,8,4,512]{3,1,2,0:T(8,128)S(1)}, u32[]{:S(2)}, u32[]{:S(2)}) collective-permute-start(f32[5,8,4,512]{3,1,2,0:T(8,128)S(1)} %get-tuple-element.116), channel_id=1, source_target_pairs={{1,0},{2,1},{3,2},{4,3},{5,4},{6,5},{7,6},{9,8},{10,9},{11,10},{12... | collective-permute-start | bytes 983048 | tf_op jit(solution)/shard_map/ppermute | solution.py:18
  22.0 6.3 %copy-start.2 = (bf16[9,8,8]{0,2,1:T(8,128)(2,1)S(1)}, bf16[9,8,8]{0,2,1:T(8,128)(2,1)}, u32[]{:S(2)}) copy-start(bf16[9,8,8]{0,2,1:T(8,128)(2,1)} %param.25) | copy-start | bytes 3460
  22.0 6.4 %copy-start.7 = (bf16[64,64]{1,0:T(8,128)(2,1)S(1)}, bf16[64,64]{1,0:T(8,128)(2,1)}, u32[]{:S(2)}) copy-start(bf16[64,64]{1,0:T(8,128)(2,1)} %param.22) | copy-start | bytes 24580
  22.4 9.5 %copy-start.3 = (bf16[64,192]{1,0:T(8,128)(2,1)S(1)}, bf16[64,192]{1,0:T(8,128)(2,1)}, u32[]{:S(2)}) copy-start(bf16[64,192]{1,0:T(8,128)(2,1)} %param.20) | copy-start | bytes 73732
  22.4 9.5 %copy-start.4 = (bf16[64,8]{0,1:T(8,128)(2,1)S(1)}, bf16[64,8]{0,1:T(8,128)(2,1)}, u32[]{:S(2)}) copy-start(bf16[64,8]{0,1:T(8,128)(2,1)} %param.23) | copy-start | bytes 3076
  22.4 9.5 %copy-start.5 = (f32[4]{0:T(128)S(1)}, f32[4]{0:T(128)}, u32[]{:S(2)}) copy-start(f32[4]{0:T(128)} %param.21) | copy-start | bytes 52
  22.4 9.5 %copy-start.6 = (bf16[8,64]{1,0:T(8,128)(2,1)S(1)}, bf16[8,64]{1,0:T(8,128)(2,1)}, u32[]{:S(2)}) copy-start(bf16[8,64]{1,0:T(8,128)(2,1)} %param.18) | copy-start | bytes 3076
  22.4 9.5 %copy-start.8 = (f32[64]{0:T(128)S(1)}, f32[64]{0:T(128)}, u32[]{:S(2)}) copy-start(f32[64]{0:T(128)} %param.19) | copy-start | bytes 772
  23.5 8.4 %all-to-all-start = ((bf16[4,2,8,8,128]{4,2,3,1,0:T(8,128)(2,1)}), bf16[4,2,8,8,128]{4,2,3,1,0:T(8,128)(2,1)S(1)}, u32[]{:S(2)}, u32[]{:S(2)}) async-start(bf16[4,2,8,8,128]{4,2,3,1,0:T(8,128)(2,1)} %pad_maximum_fusion.14), calls=%async_computation | async-start | bytes 262144 | tf_op jit(solution)/shard_map/all_to_all | solution.py:143
  54.9 3.7 %copy-start = (bf16[256,4,8,8]{3,2,1,0:T(8,128)(2,1)S(1)}, bf16[256,4,8,8]{3,2,1,0:T(8,128)(2,1)}, u32[]{:S(2)}) copy-start(bf16[256,4,8,8]{3,2,1,0:T(8,128)(2,1)} %copy.205) | copy-start | bytes 393220 | tf_op jit(solution)/shard_map/while
  88.7 3.7 %copy-start = (bf16[256,4,8,8]{3,2,1,0:T(8,128)(2,1)S(1)}, bf16[256,4,8,8]{3,2,1,0:T(8,128)(2,1)}, u32[]{:S(2)}) copy-start(bf16[256,4,8,8]{3,2,1,0:T(8,128)(2,1)} %copy.205) | copy-start | bytes 393220 | tf_op jit(solution)/shard_map/while
  122.5 3.7 %copy-start = (bf16[256,4,8,8]{3,2,1,0:T(8,128)(2,1)S(1)}, bf16[256,4,8,8]{3,2,1,0:T(8,128)(2,1)}, u32[]{:S(2)}) copy-start(bf16[256,4,8,8]{3,2,1,0:T(8,128)(2,1)} %copy.205) | copy-start | bytes 393220 | tf_op jit(solution)/shard_map/while
  156.4 3.7 %copy-start = (bf16[256,4,8,8]{3,2,1,0:T(8,128)(2,1)S(1)}, bf16[256,4,8,8]{3,2,1,0:T(8,128)(2,1)}, u32[]{:S(2)}) copy-start(bf16[256,4,8,8]{3,2,1,0:T(8,128)(2,1)} %copy.205) | copy-start | bytes 393220 | tf_op jit(solution)/shard_map/while
  167.6 5.0 %collective-permute-start.2 = (bf16[8,8,8,4]{3,1,2,0:T(8,128)(2,1)S(1)}, bf16[8,8,8,4]{3,1,2,0:T(8,128)(2,1)S(1)}, u32[]{:S(2)}, u32[]{:S(2)}) collective-permute-start(bf16[8,8,8,4]{3,1,2,0:T(8,128)(2,1)S(1)} %get-tuple-element.127), channel_id=1, source_target_pairs={{0,8},{8,16},{16,24},{1,9},{9,17},{17,25},{2,10},{10,18},{18,26},{... | collective-permute-start | bytes 12296 | tf_op jit(solution)/shard_map/ppermute | solution.py:15
  170.5 6.3 %collective-permute-start.3 = (bf16[8,8,8,4]{3,1,2,0:T(8,128)(2,1)S(1)}, bf16[8,8,8,4]{3,1,2,0:T(8,128)(2,1)S(1)}, u32[]{:S(2)}, u32[]{:S(2)}) collective-permute-start(bf16[8,8,8,4]{3,1,2,0:T(8,128)(2,1)S(1)} %get-tuple-element.128), channel_id=1, source_target_pairs={{8,0},{16,8},{24,16},{9,1},{17,9},{25,17},{10,2},{18,10},{26,18},{... | collective-permute-start | bytes 12296 | tf_op jit(solution)/shard_map/ppermute | solution.py:18
  177.0 6.0 %collective-permute-start.4 = (bf16[8,8,4,136]{3,1,2,0:T(8,128)(2,1)S(1)}, bf16[8,8,4,136]{3,1,2,0:T(8,128)(2,1)S(1)}, u32[]{:S(2)}, u32[]{:S(2)}) collective-permute-start(bf16[8,8,4,136]{3,1,2,0:T(8,128)(2,1)S(1)} %get-tuple-element.123), channel_id=1, source_target_pairs={{0,1},{1,2},{2,3},{3,4},{4,5},{5,6},{6,7},{8,9},{9,10},{10,11},{11... | collective-permute-start | bytes 208904 | tf_op jit(solution)/shard_map/ppermute | solution.py:15
  181.1 6.4 %collective-permute-start.5 = (bf16[8,8,4,136]{3,1,2,0:T(8,128)(2,1)S(1)}, bf16[8,8,4,136]{3,1,2,0:T(8,128)(2,1)S(1)}, u32[]{:S(2)}, u32[]{:S(2)}) collective-permute-start(bf16[8,8,4,136]{3,1,2,0:T(8,128)(2,1)S(1)} %get-tuple-element.124), channel_id=1, source_target_pairs={{1,0},{2,1},{3,2},{4,3},{5,4},{6,5},{7,6},{9,8},{10,9},{11,10},{12... | collective-permute-start | bytes 208904 | tf_op jit(solution)/shard_map/ppermute | solution.py:18
  189.6 5.0 %collective-permute-start.6 = (bf16[8,8,8,4]{3,1,2,0:T(8,128)(2,1)S(1)}, bf16[8,8,8,4]{3,1,2,0:T(8,128)(2,1)S(1)}, u32[]{:S(2)}, u32[]{:S(2)}) collective-permute-start(bf16[8,8,8,4]{3,1,2,0:T(8,128)(2,1)S(1)} %get-tuple-element.125), channel_id=1, source_target_pairs={{0,8},{8,16},{16,24},{1,9},{9,17},{17,25},{2,10},{10,18},{18,26},{... | collective-permute-start | bytes 12296 | tf_op jit(solution)/shard_map/ppermute | solution.py:15
  192.6 6.3 %collective-permute-start.7 = (bf16[8,8,8,4]{3,1,2,0:T(8,128)(2,1)S(1)}, bf16[8,8,8,4]{3,1,2,0:T(8,128)(2,1)S(1)}, u32[]{:S(2)}, u32[]{:S(2)}) collective-permute-start(bf16[8,8,8,4]{3,1,2,0:T(8,128)(2,1)S(1)} %get-tuple-element.126), channel_id=1, source_target_pairs={{8,0},{16,8},{24,16},{9,1},{17,9},{25,17},{10,2},{18,10},{26,18},{... | collective-permute-start | bytes 12296 | tf_op jit(solution)/shard_map/ppermute | solution.py:18
  199.1 7.8 %collective-permute-start.8 = (bf16[8,8,4,136]{3,1,2,0:T(8,128)(2,1)S(1)}, bf16[8,8,4,136]{3,1,2,0:T(8,128)(2,1)S(1)}, u32[]{:S(2)}, u32[]{:S(2)}) collective-permute-start(bf16[8,8,4,136]{3,1,2,0:T(8,128)(2,1)S(1)} %get-tuple-element.121), channel_id=1, source_target_pairs={{0,1},{1,2},{2,3},{3,4},{4,5},{5,6},{6,7},{8,9},{9,10},{10,11},{11... | collective-permute-start | bytes 208904 | tf_op jit(solution)/shard_map/ppermute | solution.py:15
  203.6 5.7 %collective-permute-start.9 = (bf16[8,8,4,136]{3,1,2,0:T(8,128)(2,1)S(1)}, bf16[8,8,4,136]{3,1,2,0:T(8,128)(2,1)S(1)}, u32[]{:S(2)}, u32[]{:S(2)}) collective-permute-start(bf16[8,8,4,136]{3,1,2,0:T(8,128)(2,1)S(1)} %get-tuple-element.122), channel_id=1, source_target_pairs={{1,0},{2,1},{3,2},{4,3},{5,4},{6,5},{7,6},{9,8},{10,9},{11,10},{12... | collective-permute-start | bytes 208904 | tf_op jit(solution)/shard_map/ppermute | solution.py:18
